TPU v7x, 512 devices: a whole 4x4x16 slice. The times are simulated.
512 devices in a mesh: expert: 8 (over y, core), mp: 64 (over x, z).
Axes of the slice: x: 4, y: 4, z: 16, core: 2. Of those that a mesh axis runs over, the one named last changes fastest.
Arguments:
- context: bfloat16 [4096, 2048], P('expert', 'mp'), may hold values from -6 to 6
- out_proj: bfloat16 [2048, 2048], P('mp'), may hold values from -1 to 1, as said below
- routes: int32 [4096, 2], P('expert'), may hold values from 0 to 7, all different within a row; in each aligned block of 512 rows (0 to 511, 512 to 1023, ...) at most 256 rows name the same one
- router_logits: float32 [4096, 2], P('expert'), may hold values from -8 to 8
- w_gate: bfloat16 [45056, 2048], P('mp', 'expert'), may hold values from -0.125 to 0.125
- w_up: bfloat16 [45056, 2048], P('mp', 'expert'), may hold values from -0.125 to 0.125
- w_down: bfloat16 [45056, 2048], P('mp', 'expert'), may hold values from -0.078125 to 0.078125
- norm_gain: float32 [2048], P('mp'), may hold values from 0.25 to 1.75
- request_order: int32 [4096], P('expert'), may hold values from 0 to 4095, each once
Outputs:
- restored: bfloat16 [4096, 2048], P('expert', 'mp')
Inputs may be any that keep to these rules, and one draw needn't show every extreme that they name: `routes`: each row names 2 different experts. Within each aligned block of 512 rows no expert is named by more than 256 rows, and in some blocks one expert is named by exactly 256 rows. `request_order`: A permutation of the 4096 token rows. `out_proj`: entries of the order of one over the square root of 2048.
All inputs are finite; a program needn't handle non-finite values.
Results may differ from a plain program's by a relative error of at most 0.0056.
Values may be sent and summed in bfloat16 or wider, within the bound.
No kernel may reach another device: no remote copies, remote signals or barrier semaphores. Data moves between devices by JAX's collectives and lax.ppermute only.
A program may use at most 64 MiB of HBM per device.

v0:
```python
import jax
import jax.numpy as jnp
from jax import lax
from jax.sharding import PartitionSpec as P

EXPERTS = 8
CAP = 256
epsilon = 1e-06


def slot_targets(routes, capacity, experts):
    flat_routes = routes.reshape(-1)
    onehot = (flat_routes[:, None] == jnp.arange(experts, dtype=jnp.int32)[None, :]).astype(
        jnp.int32
    )
    earlier = jnp.cumsum(onehot, axis=0) - onehot
    slot_index = jnp.sum(earlier * onehot, axis=1)
    return flat_routes * capacity + slot_index


def shards(
    context, out_proj, routes, router_logits, w_gate, w_up, w_down, norm_gain, request_order
):
    tok_rows = context.shape[0]
    feat_local = context.shape[1]
    model_width = out_proj.shape[1]
    mp_count = lax.axis_size("mp")
    copies = mp_count // EXPERTS
    capacity = CAP
    top_k = routes.shape[1]
    attended = jnp.einsum(
        "td,cd->tc",
        lax.all_gather(context, "mp", axis=1, tiled=True),
        out_proj,
        preferred_element_type=jnp.float32,
    ).astype(jnp.bfloat16)
    destination = slot_targets(routes, capacity, EXPERTS)
    source_rows = jnp.repeat(jnp.arange(tok_rows, dtype=jnp.int32), top_k)
    slotted = (
        jnp.zeros((EXPERTS * capacity, feat_local), jnp.bfloat16)
        .at[destination]
        .set(attended[source_rows])
    )
    slotted = jnp.repeat(slotted.reshape(EXPERTS, capacity, feat_local), copies, axis=0)
    outgoing = slotted.transpose(1, 0, 2).reshape(capacity, mp_count * feat_local)
    inbox_rows = lax.all_to_all(outgoing, "mp", split_axis=1, concat_axis=1, tiled=True)
    gate_next = jnp.einsum(
        "rd,hd->rh",
        inbox_rows,
        lax.all_gather(w_gate, "expert", axis=1, tiled=True),
        preferred_element_type=jnp.float32,
    )
    up_next = jnp.einsum(
        "rd,hd->rh",
        inbox_rows,
        lax.all_gather(w_up, "expert", axis=1, tiled=True),
        preferred_element_type=jnp.float32,
    )
    activated = (jax.nn.silu(gate_next) * up_next).astype(jnp.bfloat16)
    partial_value = jnp.dot(
        activated,
        lax.all_gather(w_down, "expert", axis=1, tiled=True),
        preferred_element_type=jnp.float32,
    )
    returned = lax.all_to_all(partial_value, "mp", split_axis=1, concat_axis=0, tiled=True)
    expert_out = jnp.sum(returned.reshape(EXPERTS, copies, capacity, feat_local), axis=1).reshape(
        EXPERTS * capacity, feat_local
    )
    picked = expert_out[destination].reshape(tok_rows, top_k, feat_local)
    weights = 1.0 / (1.0 + jnp.exp(router_logits[:, ::-1] - router_logits))
    branch = jnp.sum(picked * weights[:, :, None], axis=1)
    combined = attended.astype(jnp.float32) + branch
    squares = lax.psum(jnp.sum(combined * combined, axis=1), "mp")
    normed = (
        combined * norm_gain[None, :] * lax.rsqrt(squares / model_width + epsilon)[:, None]
    ).astype(jnp.bfloat16)
    everyone = lax.all_gather(normed, "expert", axis=0, tiled=True)
    return everyone[request_order]


def solution(mesh):
    placed = (
        P("expert", "mp"),
        P("mp", None),
        P("expert", None),
        P("expert", None),
        P("mp", "expert"),
        P("mp", "expert"),
        P("mp", "expert"),
        P("mp"),
        P("expert"),
    )
    return jax.shard_map(
        shards, mesh=mesh, in_specs=placed, out_specs=P("expert", "mp"), check_vma=False
    )
```

profile of v0, /device:TPU:1, one launch (start us, length us, event | category | flops | bytes accessed | tf_op | source)
XLA Modules:
  0.0 565.7 jit_solution(14208333560372502879)
XLA Ops:
  6.5 0.7 all-gather.5.cloned.1.call-update
  7.3 0.7 all-gather.7.cloned.1.call-update
  9.3 0.8 copy.42
  10.5 0.7 broadcast_multiply_fusion
  11.2 2.3 reduce-window.6
  14.6 133.1 %all-gather.5.cloned.1.call-done = bf16[512,2048]{0,1:T(8,128)(2,1)} async-done(((bf16[512,32]{0,1:T(8,128)(2,1)}), bf16[512,2048]{0,1:T(8,128)(2,1)}) %all-gather.5.cloned.1.call-update) | async-done | bytes 2097168 | tf_op jit(solution)/shard_map/all_gather | solution.py:33
  147.7 2.0 convolution_convert_fusion
  149.9 6.4 %scatter_custom_fusion = bf16[2048,32]{1,0:T(8,128)(2,1)S(1)} fusion(s32[1024]{0:T(1024)S(1)} %bitcast.48, bf16[512,32]{1,0:T(8,128)(2,1)S(1)} %copy.44, s32[1024]{0:T(1024)S(1)} %broadcast_clamp_fusion.1, bf16[]{:T(256)} %constant.10.clone.1), kind=kCustom, calls=%fused_computation.16 | custom fusion | bytes 131074 | tf_op jit(solution)/shard_map/scatter | solution.py:42
  156.5 1.2 broadcast_in_dim.10
  157.7 8.8 %all-to-all-start = ((bf16[256,64,32]{0,2,1:T(8,128)(2,1)}), bf16[256,64,32]{0,2,1:T(8,128)(2,1)S(1)}, u32[]{:S(2)}, u32[]{:S(2)}) async-start(bf16[256,64,32]{0,2,1:T(8,128)(2,1)} %bitcast.6), calls=%async_computation | async-start | bytes 2097152 | tf_op jit(solution)/shard_map/all_to_all | solution.py:46
  166.5 26.9 %all-gather.7.cloned.1.call-done = bf16[704,2048]{1,0:T(8,128)(2,1)} async-done(((bf16[704,256]{1,0:T(8,128)(2,1)}), bf16[704,2048]{1,0:T(8,128)(2,1)}) %all-gather.7.cloned.1.call-update) | async-done | bytes 2883600 | tf_op jit(solution)/shard_map/all_gather | solution.py:50
  193.4 12.3 %all-to-all-done = bf16[256,64,32]{0,2,1:T(8,128)(2,1)S(1)} async-done(((bf16[256,64,32]{0,2,1:T(8,128)(2,1)}), bf16[256,64,32]{0,2,1:T(8,128)(2,1)S(1)}, u32[]{:S(2)}, u32[]{:S(2)}) %all-to-all-start) | async-done | bytes 1048608 | tf_op jit(solution)/shard_map/all_to_all | solution.py:46
  205.6 2.7 fusion.16
  208.4 26.4 %all-gather.11.cloned.1.call-done = bf16[704,2048]{1,0:T(8,128)(2,1)} async-done(((bf16[704,256]{1,0:T(8,128)(2,1)}), bf16[704,2048]{1,0:T(8,128)(2,1)}) %all-gather.11.cloned.1.call-update) | async-done | bytes 2883600 | tf_op jit(solution)/shard_map/all_gather | solution.py:62
  234.8 41.3 %all-gather.9.cloned.1.call-done = bf16[704,2048]{1,0:T(8,128)(2,1)} async-done(((bf16[704,256]{1,0:T(8,128)(2,1)}), bf16[704,2048]{1,0:T(8,128)(2,1)}) %all-gather.9.cloned.1.call-update) | async-done | bytes 2883600 | tf_op jit(solution)/shard_map/all_gather | solution.py:56
  276.1 7.2 %fusion.1 = f32[256,2048]{0,1:T(8,128)} fusion(bf16[704,2048]{1,0:T(8,128)(2,1)} %all-gather.11.cloned.1.call-done, bf16[704,2048]{1,0:T(8,128)(2,1)} %all-gather.9.cloned.1.call-done, bf16[256,2048]{0,1:T(8,128)(2,1)S(1)} %bitcast.46, f32[256,704]{0,1:T(8,128)S(1)} %fusion.16), kind=kOutput, calls=%fused_computation.8 | convolution fusion | flops 1477476352 | bytes 9633792 | tf_op jit(solution)/shard_map/dot_general | solution.py:60
  283.4 15.6 %all-to-all-start.1 = ((f32[256,64,32]{0,2,1:T(8,128)}), f32[256,64,32]{0,2,1:T(8,128)S(1)}, u32[]{:S(2)}, u32[]{:S(2)}) async-start(f32[256,64,32]{0,2,1:T(8,128)} %bitcast.43), calls=%async_computation.1 | async-start | bytes 4194304 | tf_op jit(solution)/shard_map/all_to_all | solution.py:65
  299.4 91.4 %all-to-all-done.1 = f32[256,64,32]{0,2,1:T(8,128)S(1)} async-done(((f32[256,64,32]{0,2,1:T(8,128)}), f32[256,64,32]{0,2,1:T(8,128)S(1)}, u32[]{:S(2)}, u32[]{:S(2)}) %all-to-all-start.1) | async-done | bytes 2097184 | tf_op jit(solution)/shard_map/all_to_all | solution.py:65
  391.3 2.8 gather_fusion
  394.1 2.8 multiply_reduce_fusion
  397.1 118.5 %psum.7 = f32[512]{0:T(512)S(1)} all-reduce(f32[512]{0:T(512)S(1)} %multiply_reduce_fusion.1), channel_id=1, replica_groups=mesh['expert'=8,'mp'=64] {'mp'}, use_global_device_ids=true, to_apply=%region_7.8 | all-reduce | flops 512 | bytes 4096 | tf_op jit(solution)/shard_map/psum | solution.py:73
  515.6 41.0 %all_gather.19 = bf16[4096,32]{0,1:T(8,128)(2,1)S(1)} all-gather(bf16[512,32]{0,1:T(8,128)(2,1)S(1)} %multiply_convert_fusion), channel_id=1, replica_groups=mesh['expert'=8,'mp'=64] {'expert'}, dimensions={0}, use_global_device_ids=true | all-gather | bytes 294912 | tf_op jit(solution)/shard_map/all_gather | solution.py:77
  557.1 1.3 gather_fusion.1
  558.4 0.7 copy.52
  (43 shorter events, 4.6 us)
Async XLA Ops:
  6.5 141.2 %copy-start = (bf16[32,2048]{1,0:T(8,128)(2,1)S(1)}, bf16[32,2048]{1,0:T(8,128)(2,1)}, u32[]{:S(2)}) copy-start(bf16[32,2048]{1,0:T(8,128)(2,1)} %param.10) | copy-start | bytes 393220
  6.5 141.2 %all-gather.5.cloned.1.call-start = ((), (), s32[]{:S(2)}) async-start(), calls=%async_computation.2 | async-start | bytes 2129920 | tf_op jit(solution)/shard_map/all_gather | solution.py:33
  7.3 186.1 %all-gather.7.cloned.1.call-start = ((), (), s32[]{:S(2)}) async-start(), calls=%async_computation.3 | async-start | bytes 3244032 | tf_op jit(solution)/shard_map/all_gather | solution.py:50
  8.0 226.8 %all-gather.11.cloned.1.call-start = ((), (), s32[]{:S(2)}) async-start(), calls=%async_computation.5 | async-start | bytes 3244032 | tf_op jit(solution)/shard_map/all_gather | solution.py:62
  8.7 267.4 %all-gather.9.cloned.1.call-start = ((), (), s32[]{:S(2)}) async-start(), calls=%async_computation.4 | async-start | bytes 3244032 | tf_op jit(solution)/shard_map/all_gather | solution.py:56
  157.7 48.0 %all-to-all-start = ((bf16[256,64,32]{0,2,1:T(8,128)(2,1)}), bf16[256,64,32]{0,2,1:T(8,128)(2,1)S(1)}, u32[]{:S(2)}, u32[]{:S(2)}) async-start(bf16[256,64,32]{0,2,1:T(8,128)(2,1)} %bitcast.6), calls=%async_computation | async-start | bytes 2097152 | tf_op jit(solution)/shard_map/all_to_all | solution.py:46
  283.4 15.7 %copy-start.1 = (f32[512,2]{0,1:T(2,128)S(1)}, f32[512,2]{0,1:T(2,128)}, u32[]{:S(2)}) copy-start(f32[512,2]{0,1:T(2,128)} %param.12) | copy-start | bytes 12292
  283.4 16.0 %copy-start.2 = (s32[512]{0:T(512)S(1)}, s32[512]{0:T(512)}, u32[]{:S(2)}) copy-start(s32[512]{0:T(512)} %param.17) | copy-start | bytes 6148
  283.4 107.4 %all-to-all-start.1 = ((f32[256,64,32]{0,2,1:T(8,128)}), f32[256,64,32]{0,2,1:T(8,128)S(1)}, u32[]{:S(2)}, u32[]{:S(2)}) async-start(f32[256,64,32]{0,2,1:T(8,128)} %bitcast.43), calls=%async_computation.1 | async-start | bytes 4194304 | tf_op jit(solution)/shard_map/all_to_all | solution.py:65
  391.3 124.3 %copy-start.3 = (f32[32]{0:T(128)S(1)}, f32[32]{0:T(128)}, u32[]{:S(2)}) copy-start(f32[32]{0:T(128)} %param.16) | copy-start | bytes 388
Sparse Core Ops, SparseCore 0:
  10.3 137.3 all-gather.4
  149.8 43.5 all-gather.6
  195.5 39.2 all-gather.10
  236.8 39.2 all-gather.8
where the time goes:
time: 566 us
  waiting for transfers between devices  334 us (59%)
  blocking collectives  159 us (28%)
  starting transfers between devices  24.5 us (4%)
  local copies, waits for them, and re-layouts  16 us (3%)
  between operations  13.4 us (2%)
  matrix products  12 us (2%)
  other arithmetic  6.35 us (1%)
    all_gather x1, waiting for transfers between devices, shards(): lax.all_gather(context, 'mp', axis=1, tiled=True)  133 us
    psum x1, blocking collectives, shards(): squares = lax.psum(jnp.sum(combined * combined, axis=1), 'mp')  118 us
    all_to_all x1, waiting for transfers between devices, shards(): lax.all_to_all(partial_value, 'mp', split_axis=1, concat_axis=0, tiled=True)  91.4 us
    all_gather x1, waiting for transfers between devices, shards(): lax.all_gather(w_up, 'expert', axis=1, tiled=True)  41.3 us
    all_gather x1, blocking collectives, shards(): everyone = lax.all_gather(normed, 'expert', axis=0, tiled=True)  41 us
    all_gather x1, waiting for transfers between devices, shards(): lax.all_gather(w_gate, 'expert', axis=1, tiled=True)  26.9 us
    all_gather x1, waiting for transfers between devices, shards(): lax.all_gather(w_down, 'expert', axis=1, tiled=True)  26.4 us
    all_to_all x1, starting transfers between devices, shards(): lax.all_to_all(partial_value, 'mp', split_axis=1, concat_axis=0, tiled=True)  15.6 us
  transfers between devices with their start and end apart: 6, of which 6 were waited for; matrix products, arithmetic and copies ran while one was open for 3% of the time, Pallas kernels for 0%

commit v1 on v0

--- a/solution.py
+++ b/solution.py
@@ -50,11 +50,25 @@
         lax.all_gather(w_gate, "expert", axis=1, tiled=True),
         preferred_element_type=jnp.float32,
     )
+
+    def _do_results(obj):
+        world_n = jax.lax.axis_size("expert")
+        rack = [(u, (u + 1) % world_n) for u in range(world_n)]
+        all_rows = [(u, (u - 1) % world_n) for u in range(world_n)]
+        ready, field_out = ([obj], [obj])
+        for _ in range(world_n // 2):
+            ready.append(jax.lax.ppermute(ready[-1], "expert", rack))
+        for _ in [*range((world_n - 1) // 2)]:
+            then = jax.lax.ppermute(field_out[-1], "expert", all_rows)
+            field_out.append(then)
+        e_now = jnp.concatenate([*ready[::-1], *field_out[1:]], axis=1)
+        small = jnp.roll(
+            e_now, shift=(jax.lax.axis_index("expert") - world_n // 2) * obj.shape[1], axis=1
+        )
+        return small
+
     up_next = jnp.einsum(
-        "rd,hd->rh",
-        inbox_rows,
-        lax.all_gather(w_up, "expert", axis=1, tiled=True),
-        preferred_element_type=jnp.float32,
+        "rd,hd->rh", inbox_rows, _do_results(w_up), preferred_element_type=jnp.float32
     )
     activated = (jax.nn.silu(gate_next) * up_next).astype(jnp.bfloat16)
     partial_value = jnp.dot(

time: 566 us -> 529 us (0.935)
  waiting for transfers between devices: 334 us -> 262 us
  starting transfers between devices: 24.5 us -> 46.2 us
  local copies, waits for them, and re-layouts: 16 us -> 28.9 us
    all_gather x1 -> x0, waiting for transfers between devices: 41.3 us -> none  [shards(): lax.all_gather(w_up, 'expert', axis=1, tiled=True)]
    all_gather x1, waiting for transfers between devices: 26.9 us -> 0.01 us  [shards(): lax.all_gather(w_gate, 'expert', axis=1, tiled=True)]
    ppermute x0 -> x7, starting transfers between devices: none -> 21.6 us  [the longest x4 19.6 us: _do_results(): ready.append(jax.lax.ppermute(ready[-1], 'expert', rack))]
    ppermute x0 -> x7, waiting for transfers between devices: none -> 21.4 us  [the longest x4 21 us: _do_results(): ready.append(jax.lax.ppermute(ready[-1], 'expert', rack))]
    all_gather x1, waiting for transfers between devices: 26.4 us -> 13 us  [shards(): lax.all_gather(w_down, 'expert', axis=1, tiled=True)]
    all_to_all x1, waiting for transfers between devices: 12.3 us -> 0.01 us  [shards(): lax.all_to_all(outgoing, 'mp', split_axis=1, concat_axis=1, tiled=True)]
    unnamed x9 -> x26, local copies, waits for them, and re-layouts: 0.85 us -> 13 us
  transfers between devices with their start and end apart: 6 -> 12, of which waited for: 6 -> 8; matrix products, arithmetic and copies ran while one was open for 3% -> 6% of each run, Pallas kernels for 0% -> 0%
where the time goes in v1:
time: 529 us
  waiting for transfers between devices  262 us (50%)
  blocking collectives  159 us (30%)
  starting transfers between devices  46.2 us (9%)
  local copies, waits for them, and re-layouts  28.9 us (5%)
  between operations  13.4 us (3%)
  matrix products  12.6 us (2%)
  other arithmetic  6.35 us (1%)
    all_gather x1, waiting for transfers between devices, shards(): lax.all_gather(context, 'mp', axis=1, tiled=True)  134 us
    psum x1, blocking collectives, shards(): squares = lax.psum(jnp.sum(combined * combined, axis=1), 'mp')  118 us
    all_to_all x1, waiting for transfers between devices, shards(): lax.all_to_all(partial_value, 'mp', split_axis=1, concat_axis=0, tiled=True)  91.4 us
    all_gather x1, blocking collectives, shards(): everyone = lax.all_gather(normed, 'expert', axis=0, tiled=True)  41 us
    ppermute x4, waiting for transfers between devices, _do_results(): ready.append(jax.lax.ppermute(ready[-1], 'expert', rack))  21 us
    ppermute x4, starting transfers between devices, _do_results(): ready.append(jax.lax.ppermute(ready[-1], 'expert', rack))  19.6 us
    all_to_all x1, starting transfers between devices, shards(): lax.all_to_all(partial_value, 'mp', split_axis=1, concat_axis=0, tiled=True)  15.5 us
    all_gather x1, waiting for transfers between devices, shards(): lax.all_gather(w_down, 'expert', axis=1, tiled=True)  13 us
  transfers between devices with their start and end apart: 12, of which 8 were waited for; matrix products, arithmetic and copies ran while one was open for 6% of the time, Pallas kernels for 0%

profile of v1, /device:TPU:1, one launch (start us, length us, event | category | flops | bytes accessed | tf_op | source)
XLA Modules:
  0.0 528.5 jit_solution(10439522784462776525)
XLA Ops:
  10.6 2.3 reduce-window.6
  14.0 133.7 %all-gather.4.cloned.1.call-done = bf16[512,2048]{0,1:T(8,128)(2,1)} async-done(((bf16[512,32]{0,1:T(8,128)(2,1)}), bf16[512,2048]{0,1:T(8,128)(2,1)}) %all-gather.4.cloned.1.call-update) | async-done | bytes 2097168 | tf_op jit(solution)/shard_map/all_gather | solution.py:33
  147.7 2.0 convolution_convert_fusion
  149.9 6.4 %scatter_custom_fusion = bf16[2048,32]{1,0:T(8,128)(2,1)S(1)} fusion(s32[1024]{0:T(1024)S(1)} %bitcast.45, bf16[512,32]{1,0:T(8,128)(2,1)S(1)} %copy.44, s32[1024]{0:T(1024)S(1)} %broadcast_clamp_fusion.1, bf16[]{:T(256)} %constant.22.clone.1), kind=kCustom, calls=%fused_computation.18 | custom fusion | bytes 131074 | tf_op jit(solution)/shard_map/scatter | solution.py:42
  156.5 1.2 broadcast_in_dim.10
  157.7 9.0 %all-to-all-start = ((bf16[256,64,32]{0,2,1:T(8,128)(2,1)}), bf16[256,64,32]{0,2,1:T(8,128)(2,1)}, u32[]{:S(2)}, u32[]{:S(2)}) async-start(bf16[256,64,32]{0,2,1:T(8,128)(2,1)} %bitcast.6), calls=%async_computation | async-start | bytes 2097152 | tf_op jit(solution)/shard_map/all_to_all | solution.py:46
  166.7 12.1 %collective-permute-start = (bf16[704,256]{1,0:T(8,128)(2,1)S(1)}, bf16[704,256]{1,0:T(8,128)(2,1)S(1)}, u32[]{:S(2)}, u32[]{:S(2)}) collective-permute-start(bf16[704,256]{1,0:T(8,128)(2,1)S(1)} %copy-done.1), channel_id=1, source_target_pairs={{0,64},{64,128},{128,192},{192,256},{256,320},{320,384},{384,448},... | collective-permute-start | bytes 1081352 | tf_op jit(solution)/shard_map/ppermute | solution.py:60
  178.9 8.2 %collective-permute-done = bf16[704,256]{1,0:T(8,128)(2,1)S(1)} collective-permute-done((bf16[704,256]{1,0:T(8,128)(2,1)S(1)}, bf16[704,256]{1,0:T(8,128)(2,1)S(1)}, u32[]{:S(2)}, u32[]{:S(2)}) %collective-permute-start) | collective-permute-done | bytes 360480 | tf_op jit(solution)/shard_map/ppermute | solution.py:60
  187.1 2.5 collective-permute-start.1
  190.5 5.5 %collective-permute-done.1 = bf16[704,256]{1,0:T(8,128)(2,1)S(1)} collective-permute-done((bf16[704,256]{1,0:T(8,128)(2,1)S(1)}, bf16[704,256]{1,0:T(8,128)(2,1)S(1)}, u32[]{:S(2)}, u32[]{:S(2)}) %collective-permute-start.1) | collective-permute-done | bytes 360480 | tf_op jit(solution)/shard_map/ppermute | solution.py:60
  196.0 2.5 collective-permute-start.2
  198.6 4.3 collective-permute-done.2
  202.9 2.5 collective-permute-start.3
  206.9 2.9 collective-permute-done.3
  222.7 3.0 fusion.27
  225.7 13.0 %all-gather.8.cloned.1.call-done = bf16[704,2048]{1,0:T(8,128)(2,1)} async-done(((bf16[704,256]{1,0:T(8,128)(2,1)}), bf16[704,2048]{1,0:T(8,128)(2,1)}) %all-gather.8.cloned.1.call-update) | async-done | bytes 2883600 | tf_op jit(solution)/shard_map/all_gather | solution.py:76
  238.7 7.6 %fusion.9 = f32[256,2048]{0,1:T(8,128)} fusion(bf16[704,2048]{1,0:T(8,128)(2,1)} %all-gather.8.cloned.1.call-done, bf16[256,2048]{0,1:T(8,128)(2,1)} %bitcast.7, bf16[704,4096]{1,0:T(8,128)(2,1)} %constant_dynamic-update-slice_fusion, s32[]{:T(128)S(6)} %select_n.40, f32[256,704]{0,1:T(8,128)S(1)} %fusion.27), kind=kOutput, calls=%fused_computation.10 | convolution fusion | flops 1477476352 | bytes 9633796 | tf_op jit(solution)/shard_map/dot_general | solution.py:74
  246.3 15.5 %all-to-all-start.1 = ((f32[256,64,32]{0,2,1:T(8,128)}), f32[256,64,32]{0,2,1:T(8,128)S(1)}, u32[]{:S(2)}, u32[]{:S(2)}) async-start(f32[256,64,32]{0,2,1:T(8,128)} %bitcast.42), calls=%async_computation.1 | async-start | bytes 4194304 | tf_op jit(solution)/shard_map/all_to_all | solution.py:79
  262.2 91.4 %all-to-all-done.1 = f32[256,64,32]{0,2,1:T(8,128)S(1)} async-done(((f32[256,64,32]{0,2,1:T(8,128)}), f32[256,64,32]{0,2,1:T(8,128)S(1)}, u32[]{:S(2)}, u32[]{:S(2)}) %all-to-all-start.1) | async-done | bytes 2097184 | tf_op jit(solution)/shard_map/all_to_all | solution.py:79
  354.1 2.8 gather_fusion
  356.9 2.8 multiply_reduce_fusion
  359.9 118.5 %psum.7 = f32[512]{0:T(512)S(1)} all-reduce(f32[512]{0:T(512)S(1)} %multiply_reduce_fusion.1), channel_id=1, replica_groups=mesh['expert'=8,'mp'=64] {'mp'}, use_global_device_ids=true, to_apply=%region_7.8 | all-reduce | flops 512 | bytes 4096 | tf_op jit(solution)/shard_map/psum | solution.py:87
  478.5 41.0 %all_gather.15 = bf16[4096,32]{0,1:T(8,128)(2,1)S(1)} all-gather(bf16[512,32]{0,1:T(8,128)(2,1)S(1)} %multiply_convert_fusion), channel_id=1, replica_groups=mesh['expert'=8,'mp'=64] {'expert'}, dimensions={0}, use_global_device_ids=true | all-gather | bytes 294912 | tf_op jit(solution)/shard_map/all_gather | solution.py:91
  519.9 1.3 gather_fusion.1
  (72 shorter events, 23.0 us)
Async XLA Ops:
  6.5 141.2 %copy-start = (bf16[32,2048]{1,0:T(8,128)(2,1)S(1)}, bf16[32,2048]{1,0:T(8,128)(2,1)}, u32[]{:S(2)}) copy-start(bf16[32,2048]{1,0:T(8,128)(2,1)} %param.10) | copy-start | bytes 393220
  6.5 160.2 %copy-start.1 = (bf16[704,256]{1,0:T(8,128)(2,1)S(1)}, bf16[704,256]{1,0:T(8,128)(2,1)}, u32[]{:S(2)}) copy-start(bf16[704,256]{1,0:T(8,128)(2,1)} %param.14) | copy-start | bytes 1081348
  6.5 141.2 %all-gather.4.cloned.1.call-start = ((), (), s32[]{:S(2)}) async-start(), calls=%async_computation.2 | async-start | bytes 2129920 | tf_op jit(solution)/shard_map/all_gather | solution.py:33
  7.3 215.4 %all-gather.6.cloned.1.call-start = ((), (), s32[]{:S(2)}) async-start(), calls=%async_computation.3 | async-start | bytes 3244032 | tf_op jit(solution)/shard_map/all_gather | solution.py:50
  8.0 230.7 %all-gather.8.cloned.1.call-start = ((), (), s32[]{:S(2)}) async-start(), calls=%async_computation.4 | async-start | bytes 3244032 | tf_op jit(solution)/shard_map/all_gather | solution.py:76
  157.7 65.0 %all-to-all-start = ((bf16[256,64,32]{0,2,1:T(8,128)(2,1)}), bf16[256,64,32]{0,2,1:T(8,128)(2,1)}, u32[]{:S(2)}, u32[]{:S(2)}) async-start(bf16[256,64,32]{0,2,1:T(8,128)(2,1)} %bitcast.6), calls=%async_computation | async-start | bytes 2097152 | tf_op jit(solution)/shard_map/all_to_all | solution.py:46
  166.7 20.4 %collective-permute-start = (bf16[704,256]{1,0:T(8,128)(2,1)S(1)}, bf16[704,256]{1,0:T(8,128)(2,1)S(1)}, u32[]{:S(2)}, u32[]{:S(2)}) collective-permute-start(bf16[704,256]{1,0:T(8,128)(2,1)S(1)} %copy-done.1), channel_id=1, source_target_pairs={{0,64},{64,128},{128,192},{192,256},{256,320},{320,384},{384,448},... | collective-permute-start | bytes 1081352 | tf_op jit(solution)/shard_map/ppermute | solution.py:60
  187.1 8.9 %collective-permute-start.1 = (bf16[704,256]{1,0:T(8,128)(2,1)S(1)}, bf16[704,256]{1,0:T(8,128)(2,1)S(1)}, u32[]{:S(2)}, u32[]{:S(2)}) collective-permute-start(bf16[704,256]{1,0:T(8,128)(2,1)S(1)} %collective-permute-done), channel_id=1, source_target_pairs={{0,64},{64,128},{128,192},{192,256},{256,320},{320,384},{384,448},... | collective-permute-start | bytes 1081352 | tf_op jit(solution)/shard_map/ppermute | solution.py:60
  189.6 8.9 %collective-permute-start.4 = (bf16[704,256]{1,0:T(8,128)(2,1)S(1)}, bf16[704,256]{1,0:T(8,128)(2,1)S(1)}, u32[]{:S(2)}, u32[]{:S(2)}) collective-permute-start(bf16[704,256]{1,0:T(8,128)(2,1)S(1)} %copy-done.1), channel_id=1, source_target_pairs={{0,448},{64,0},{128,64},{192,128},{256,192},{320,256},{384,320},{4... | collective-permute-start | bytes 1081352 | tf_op jit(solution)/shard_map/ppermute | solution.py:62
  196.0 6.9 %collective-permute-start.2 = (bf16[704,256]{1,0:T(8,128)(2,1)S(1)}, bf16[704,256]{1,0:T(8,128)(2,1)S(1)}, u32[]{:S(2)}, u32[]{:S(2)}) collective-permute-start(bf16[704,256]{1,0:T(8,128)(2,1)S(1)} %collective-permute-done.1), channel_id=1, source_target_pairs={{0,64},{64,128},{128,192},{192,256},{256,320},{320,384},{384,448},... | collective-permute-start | bytes 1081352 | tf_op jit(solution)/shard_map/ppermute | solution.py:60
  198.5 7.3 %collective-permute-start.5 = (bf16[704,256]{1,0:T(8,128)(2,1)S(1)}, bf16[704,256]{1,0:T(8,128)(2,1)S(1)}, u32[]{:S(2)}, u32[]{:S(2)}) collective-permute-start(bf16[704,256]{1,0:T(8,128)(2,1)S(1)} %collective-permute-done.4), channel_id=1, source_target_pairs={{0,448},{64,0},{128,64},{192,128},{256,192},{320,256},{384,320},{4... | collective-permute-start | bytes 1081352 | tf_op jit(solution)/shard_map/ppermute | solution.py:62
  202.9 6.9 %collective-permute-start.3 = (bf16[704,256]{1,0:T(8,128)(2,1)S(1)}, bf16[704,256]{1,0:T(8,128)(2,1)S(1)}, u32[]{:S(2)}, u32[]{:S(2)}) collective-permute-start(bf16[704,256]{1,0:T(8,128)(2,1)S(1)} %collective-permute-done.2), channel_id=1, source_target_pairs={{0,64},{64,128},{128,192},{192,256},{256,320},{320,384},{384,448},... | collective-permute-start | bytes 1081352 | tf_op jit(solution)/shard_map/ppermute | solution.py:60
  205.8 9.6 %collective-permute-start.6 = (bf16[704,256]{1,0:T(8,128)(2,1)S(1)}, bf16[704,256]{1,0:T(8,128)(2,1)S(1)}, u32[]{:S(2)}, u32[]{:S(2)}) collective-permute-start(bf16[704,256]{1,0:T(8,128)(2,1)S(1)} %collective-permute-done.5), channel_id=1, source_target_pairs={{0,448},{64,0},{128,64},{192,128},{256,192},{320,256},{384,320},{4... | collective-permute-start | bytes 1081352 | tf_op jit(solution)/shard_map/ppermute | solution.py:62
  225.7 36.2 %copy-start.2 = (f32[512,2]{0,1:T(2,128)S(1)}, f32[512,2]{0,1:T(2,128)}, u32[]{:S(2)}) copy-start(f32[512,2]{0,1:T(2,128)} %param.12) | copy-start | bytes 12292
  225.7 36.5 %copy-start.3 = (s32[512]{0:T(512)S(1)}, s32[512]{0:T(512)}, u32[]{:S(2)}) copy-start(s32[512]{0:T(512)} %param.17) | copy-start | bytes 6148
  246.3 107.3 %all-to-all-start.1 = ((f32[256,64,32]{0,2,1:T(8,128)}), f32[256,64,32]{0,2,1:T(8,128)S(1)}, u32[]{:S(2)}, u32[]{:S(2)}) async-start(f32[256,64,32]{0,2,1:T(8,128)} %bitcast.42), calls=%async_computation.1 | async-start | bytes 4194304 | tf_op jit(solution)/shard_map/all_to_all | solution.py:79
  261.9 216.5 %copy-start.4 = (f32[32]{0:T(128)S(1)}, f32[32]{0:T(128)}, u32[]{:S(2)}) copy-start(f32[32]{0:T(128)} %param.16) | copy-start | bytes 388
Sparse Core Ops, SparseCore 0:
  10.3 137.3 all-gather.3
  149.8 46.8 all-gather.5
  198.8 39.8 all-gather.7
